TPU v7x, 32 devices: a whole 2x2x4 slice. The times are simulated.
32 devices in a mesh: dp: 8 (over z, y), region: 4 (over x, core).
Axes of the slice: x: 2, y: 2, z: 4, core: 2. Of those that a mesh axis runs over, the one named last changes fastest.
Arguments:
- travel_times: float32 [512, 128], P('dp'), may hold values from -60 to 60
- sensitivity: bfloat16 [512, 8, 128, 128], P('dp', 'region'), may hold values from -0.1875 to 0.1875
- tile_blocks: int32 [512, 8], P('dp', 'region'), may hold values from 0 to 1023
- face_blocks: int32 [1024, 2], P(('dp', 'region')), may hold values from 0 to 1023, as said below
- face_weights: float32 [1024, 128], P(('dp', 'region')), may hold values from 0.2 to 2
- face_count: int32 [32], P(('dp', 'region')), may hold values from 8 to 32, as said below
Outputs:
- solution: float32 [1024, 128], P('region')
Inputs may be any that keep to these rules, and one draw needn't show every extreme that they name: `face_blocks`: the first block of a face lies in the region of the device that holds the face, the second in that region or in the region one step up or down, the regions closing into a loop. `face_count`: entry k counts the faces in use among the 32 rows held by device k of dp+region; they are its first rows; some device holds 32.
All inputs are finite; a program needn't handle non-finite values.
Results may differ from a plain program's by a relative error of at most 0.0025.
The roundings to bfloat16 on the way count: a program that leaves them out, or rounds other values in their place, can miss the bound.
Values may be sent and summed in bfloat16 or wider, within the bound.
No kernel may reach another device: no remote copies, remote signals or barrier semaphores. Data moves between devices by JAX's collectives and lax.ppermute only.
A program may use at most 64 MiB of HBM per device.

v0:
```python
import jax
import jax.numpy as jnp
from jax import lax
from jax.sharding import PartitionSpec as P

ITERS = 2
NB_DEV = 256
smooth_weight = 1.0


def reduce_partials(partials):
    summed = lax.psum(partials, ("dp", "region"))
    return lax.dynamic_slice_in_dim(summed, lax.axis_index("region") * NB_DEV, NB_DEV, 0)


def piece_squares(piece):
    local_sq = jnp.sum(piece * piece)
    return lax.psum(local_sq, "region")


def model_field(piece):
    slab_half = piece.astype(jnp.bfloat16)
    return lax.all_gather(slab_half, "region", axis=0, tiled=True)


def left_squares(ray_sq, face_sq):
    return lax.psum(ray_sq, "dp") + lax.psum(face_sq, ("dp", "region"))


def local(travel_times, sensitivity, tile_blocks, face_blocks, face_weights, face_count):
    model_rows = NB_DEV * lax.axis_size("region")
    live_mask = (jnp.arange(face_blocks.shape[0]) < face_count[0]).astype(jnp.float32)
    face_scale = smooth_weight * face_weights * live_mask[:, None]
    first_block = face_blocks[:, 0]
    second_block = face_blocks[:, 1]
    flat_blocks = tile_blocks.reshape(-1)

    def transposed(left_rays, left_faces):
        rays_half = left_rays.astype(jnp.bfloat16)
        contrib = jnp.einsum(
            "tsrb,tr->tsb", sensitivity, rays_half, preferred_element_type=jnp.float32
        )
        contrib_rows = contrib.reshape(-1, contrib.shape[-1])
        face_term = face_scale * left_faces
        partials = jax.ops.segment_sum(contrib_rows, flat_blocks, num_segments=model_rows)
        partials = partials + jax.ops.segment_sum(face_term, first_block, num_segments=model_rows)
        partials = partials - jax.ops.segment_sum(face_term, second_block, num_segments=model_rows)
        return reduce_partials(partials)

    beta_value = jnp.sqrt(
        left_squares(jnp.sum(travel_times * travel_times), jnp.zeros((), jnp.float32))
    )
    left_rays = travel_times / beta_value
    left_faces = jnp.zeros(face_weights.shape, jnp.float32)
    right_vector = transposed(left_rays, left_faces)
    alpha_value = jnp.sqrt(piece_squares(right_vector))
    right_vector = right_vector / alpha_value
    direction = right_vector
    solution = jnp.zeros_like(right_vector)
    phi_bar = beta_value
    rho_bar = alpha_value
    for iteration in range(ITERS):
        full_model = model_field(right_vector)
        picked = full_model[tile_blocks]
        partial_value = jnp.einsum(
            "tsrb,tsb->tr", sensitivity, picked, preferred_element_type=jnp.float32
        )
        ray_pred = lax.psum(partial_value.astype(jnp.bfloat16), "region").astype(jnp.float32)
        face_pred = face_scale * (
            full_model[first_block].astype(jnp.float32)
            - full_model[second_block].astype(jnp.float32)
        )
        ray_pred, face_pred = (ray_pred, face_pred)
        left_rays = ray_pred - alpha_value * left_rays
        left_faces = face_pred - alpha_value * left_faces
        beta_value = jnp.sqrt(
            left_squares(jnp.sum(left_rays * left_rays), jnp.sum(left_faces * left_faces))
        )
        left_rays = left_rays / beta_value
        left_faces = left_faces / beta_value
        last_turn = iteration + 1 == ITERS
        if not last_turn:
            right_vector = transposed(left_rays, left_faces) - beta_value * right_vector
            alpha_new = jnp.sqrt(piece_squares(right_vector))
            right_vector = right_vector / alpha_new
        rho_value = jnp.sqrt(rho_bar * rho_bar + beta_value * beta_value)
        cosine = rho_bar / rho_value
        sine_value = beta_value / rho_value
        phi_value = cosine * phi_bar
        phi_bar = sine_value * phi_bar
        solution = solution + phi_value / rho_value * direction
        if not last_turn:
            rho_bar = -cosine * alpha_new
            direction = right_vector - sine_value * alpha_new / rho_value * direction
            alpha_value = alpha_new
    return solution


def solution(mesh):
    in_specs = (
        P("dp", None),
        P("dp", "region", None, None),
        P("dp", "region"),
        P(("dp", "region"), None),
        P(("dp", "region"), None),
        P(("dp", "region")),
    )
    out_specs = P("region", None)
    return jax.shard_map(local, mesh=mesh, in_specs=in_specs, out_specs=out_specs, check_vma=False)
```

profile of v0, /device:TPU:12, one launch (start us, length us, event | category | flops | bytes accessed | tf_op | source)
XLA Modules:
  0.0 539.1 jit_solution(2553015749312402894)
XLA Ops:
  7.3 0.8 copy.9
  8.7 1.4 multiply_reduce_fusion.4
  10.2 15.8 %psum.84 = f32[]{:T(128)} all-reduce(f32[]{:T(128)} %multiply_reduce_fusion.4), channel_id=1, replica_groups=mesh['dp'=8,'region'=4] {'dp'}, use_global_device_ids=true, to_apply=%region_1.0 | all-reduce | flops 1 | bytes 8 | tf_op jit(solution)/shard_map/psum | solution.py:27
  26.0 46.4 %psum.85 = f32[]{:T(128)} all-reduce(f32[]{:T(128)} %constant.5.clone.1), channel_id=1, replica_groups=mesh['dp'=8,'region'=4] {'dp','region'}, use_global_device_ids=true, to_apply=%region_2.0 | all-reduce | flops 1 | bytes 8 | tf_op jit(solution)/shard_map/psum | solution.py:27
  74.6 0.8 multiply_multiply_fusion.1
  75.4 1.1 scatter_custom_fusion.1
  76.5 2.8 fusion.21
  79.3 1.3 scatter_custom_fusion
  80.6 0.9 sub.30
  81.8 126.7 %all-reduce.3.cloned.1.call-done = f32[1024,128]{1,0:T(8,128)} async-done(((f32[1024,128]{1,0:T(8,128)}), f32[1024,128]{1,0:T(8,128)}) %all-reduce.3.cloned.1.call-update) | async-done | bytes 524304 | tf_op jit(solution)/shard_map/psum | solution.py:12
  208.6 1.5 multiply_reduce_fusion.1
  210.1 6.3 %psum.87 = f32[]{:T(128)} all-reduce(f32[]{:T(128)} %multiply_reduce_fusion.1), channel_id=1, replica_groups=mesh['dp'=8,'region'=4] {'region'}, use_global_device_ids=true, to_apply=%region_7.0 | all-reduce | flops 1 | bytes 8 | tf_op jit(solution)/shard_map/psum | solution.py:18
  217.1 0.9 fusion.26
  218.0 5.8 %all_gather.6 = bf16[1024,128]{1,0:T(8,128)(2,1)S(1)} all-gather(bf16[256,128]{1,0:T(8,128)(2,1)S(1)} %fusion.26), channel_id=1, replica_groups=mesh['dp'=8,'region'=4] {'region'}, dimensions={0}, use_global_device_ids=true | all-gather | bytes 327680 | tf_op jit(solution)/shard_map/all_gather | solution.py:23
  224.5 3.4 fusion.16
  227.9 10.7 %psum.88 = bf16[64,128]{1,0:T(8,128)(2,1)S(1)} all-reduce(bf16[64,128]{1,0:T(8,128)(2,1)S(1)} %convert_element_type.46), channel_id=1, replica_groups=mesh['dp'=8,'region'=4] {'region'}, use_global_device_ids=true, to_apply=%region_8.0 | all-reduce | flops 8192 | bytes 32768 | tf_op jit(solution)/shard_map/psum | solution.py:68
  241.2 16.7 %psum.89 = f32[]{:T(128)} all-reduce(f32[]{:T(128)} %multiply_reduce_fusion.3), channel_id=1, replica_groups=mesh['dp'=8,'region'=4] {'dp'}, use_global_device_ids=true, to_apply=%region_10.0 | all-reduce | flops 1 | bytes 8 | tf_op jit(solution)/shard_map/psum | solution.py:27
  257.9 43.8 %psum.90 = f32[]{:T(128)} all-reduce(f32[]{:T(128)} %multiply_reduce_fusion.6), channel_id=1, replica_groups=mesh['dp'=8,'region'=4] {'dp','region'}, use_global_device_ids=true, to_apply=%region_12.0 | all-reduce | flops 1 | bytes 8 | tf_op jit(solution)/shard_map/psum | solution.py:27
  303.2 2.8 fusion.19
  306.0 0.8 scatter_custom_fusion.3
  306.9 1.3 scatter_custom_fusion.2
  308.2 0.9 sub.34
  309.2 126.8 %all-reduce.5.cloned.1.call-done = f32[1024,128]{1,0:T(8,128)} async-done(((f32[1024,128]{1,0:T(8,128)}), f32[1024,128]{1,0:T(8,128)}) %all-reduce.5.cloned.1.call-update) | async-done | bytes 524304 | tf_op jit(solution)/shard_map/psum | solution.py:12
  436.0 1.6 multiply_reduce_fusion
  437.6 6.3 %psum.92 = f32[]{:T(128)} all-reduce(f32[]{:T(128)} %multiply_reduce_fusion), channel_id=1, replica_groups=mesh['dp'=8,'region'=4] {'region'}, use_global_device_ids=true, to_apply=%region_17.0 | all-reduce | flops 1 | bytes 8 | tf_op jit(solution)/shard_map/psum | solution.py:18
  444.6 0.9 fusion.18
  445.6 5.8 %all_gather.7 = bf16[1024,128]{1,0:T(8,128)(2,1)S(1)} all-gather(bf16[256,128]{1,0:T(8,128)(2,1)S(1)} %fusion.18), channel_id=1, replica_groups=mesh['dp'=8,'region'=4] {'region'}, dimensions={0}, use_global_device_ids=true | all-gather | bytes 327680 | tf_op jit(solution)/shard_map/all_gather | solution.py:23
  453.3 3.4 fusion.14
  456.7 10.6 %psum.93 = bf16[64,128]{1,0:T(8,128)(2,1)S(1)} all-reduce(bf16[64,128]{1,0:T(8,128)(2,1)S(1)} %convert_element_type.52), channel_id=1, replica_groups=mesh['dp'=8,'region'=4] {'region'}, use_global_device_ids=true, to_apply=%region_18.0 | all-reduce | flops 8192 | bytes 32768 | tf_op jit(solution)/shard_map/psum | solution.py:68
  467.9 16.7 %psum.94 = f32[]{:T(128)} all-reduce(f32[]{:T(128)} %multiply_reduce_fusion.2), channel_id=1, replica_groups=mesh['dp'=8,'region'=4] {'dp'}, use_global_device_ids=true, to_apply=%region_20.0 | all-reduce | flops 1 | bytes 8 | tf_op jit(solution)/shard_map/psum | solution.py:27
  485.4 43.8 %psum.95 = f32[]{:T(128)} all-reduce(f32[]{:T(128)} %multiply_reduce_fusion.5), channel_id=1, replica_groups=mesh['dp'=8,'region'=4] {'dp','region'}, use_global_device_ids=true, to_apply=%region_22.0 | all-reduce | flops 1 | bytes 8 | tf_op jit(solution)/shard_map/psum | solution.py:27
  530.7 1.6 multiply_add_fusion
  (36 shorter events, 8.7 us)
Async XLA Ops:
  6.5 75.0 %copy-start.3 = (s32[64,2]{0,1:T(2,128)S(1)}, s32[64,2]{0,1:T(2,128)}, u32[]{:S(2)}) copy-start(s32[64,2]{0,1:T(2,128)} %param.8) | copy-start | bytes 1540
  6.5 202.0 %all-reduce.3.cloned.1.call-start = ((), (), s32[]{:S(2)}) async-start(), calls=%async_computation | async-start | bytes 1048576 | tf_op jit(solution)/shard_map/psum | solution.py:12
  79.3 159.3 %copy-start.1 = (f32[64,128]{1,0:T(8,128)S(1)}, f32[64,128]{1,0:T(8,128)}, u32[]{:S(2)}) copy-start(f32[64,128]{1,0:T(8,128)} %param.6) | copy-start | bytes 98308
  79.3 161.1 %copy-start.2 = (f32[32,128]{1,0:T(8,128)S(1)}, f32[32,128]{1,0:T(8,128)}, u32[]{:S(2)}) copy-start(f32[32,128]{1,0:T(8,128)} %param.10) | copy-start | bytes 49156
  81.5 354.5 %all-reduce.5.cloned.1.call-start = ((), (), s32[]{:S(2)}) async-start(), calls=%async_computation.1 | async-start | bytes 1048576 | tf_op jit(solution)/shard_map/psum | solution.py:12
  227.9 208.1 %copy-start = (f32[1024,128]{1,0:T(8,128)S(1)}, f32[1024,128]{1,0:T(8,128)}, u32[]{:S(2)}) copy-start(f32[1024,128]{1,0:T(8,128)} %all-reduce.3.cloned.1.call-done) | copy-start | bytes 1572868
Sparse Core Ops, SparseCore 0:
  81.6 126.9 all-reduce.2
  309.2 126.7 all-reduce.4
where the time goes:
time: 540 us; the launch traced here: 539 us
  waiting for transfers between devices  254 us (47%)
  blocking collectives  229 us (42%)
  between operations  20.1 us (4%)
  other arithmetic  19.3 us (4%)
  matrix products  12.4 us (2%)
    psum x2, waiting for transfers between devices, reduce_partials(): summed = lax.psum(partials, ('dp', 'region'))  254 us
    psum x6, blocking collectives, left_squares(): return lax.psum(ray_sq, 'dp') + lax.psum(face_sq, ('dp', 'region'))  183 us
    psum x2, blocking collectives, local(): lax.psum(partial_value.astype(jnp.bfloat16), 'region').astype(jnp.float32)  21.3 us
    psum x2, blocking collectives, piece_squares(): return lax.psum(local_sq, 'region')  12.6 us
    all_gather x2, blocking collectives, model_field(): return lax.all_gather(slab_half, 'region', axis=0, tiled=True)  11.6 us
  transfers between devices with their start and end apart: 2, of which 2 were waited for; matrix products, arithmetic and copies ran while one was open for 0% of the time, Pallas kernels for 0%

commit v1 on v0

--- a/solution.py
+++ b/solution.py
@@ -9,7 +9,7 @@
 
 
 def reduce_partials(partials):
-    summed = lax.psum(partials, ("dp", "region"))
+    summed = lax.psum(lax.psum(partials, "region"), "dp")
     return lax.dynamic_slice_in_dim(summed, lax.axis_index("region") * NB_DEV, NB_DEV, 0)
 
 

time: 540 us -> 503 us (0.931)
  waiting for transfers between devices: 254 us -> 214 us
    psum x2 -> x4, waiting for transfers between devices: 254 us -> 214 us  [reduce_partials(): summed = lax.psum(lax.psum(partials, 'region'), 'dp')]
  transfers between devices with their start and end apart: 2 -> 4, of which waited for: 2 -> 4; matrix products, arithmetic and copies ran while one was open for 0% -> 0% of each run, Pallas kernels for 0% -> 0%
where the time goes in v1:
time: 503 us; the launch traced here: 502 us
  blocking collectives  230 us (46%)
  waiting for transfers between devices  214 us (43%)
  between operations  19.8 us (4%)
  other arithmetic  19.3 us (4%)
  matrix products  12.4 us (2%)
    psum x4, waiting for transfers between devices, reduce_partials(): summed = lax.psum(lax.psum(partials, 'region'), 'dp')  214 us
    psum x6, blocking collectives, left_squares(): return lax.psum(ray_sq, 'dp') + lax.psum(face_sq, ('dp', 'region'))  183 us
    psum x2, blocking collectives, local(): lax.psum(partial_value.astype(jnp.bfloat16), 'region').astype(jnp.float32)  22.9 us
    psum x2, blocking collectives, piece_squares(): return lax.psum(local_sq, 'region')  12.6 us
    all_gather x2, blocking collectives, model_field(): return lax.all_gather(slab_half, 'region', axis=0, tiled=True)  12 us
  transfers between devices with their start and end apart: 4, of which 4 were waited for; matrix products, arithmetic and copies ran while one was open for 0% of the time, Pallas kernels for 0%

profile of v1, /device:TPU:12, one launch (start us, length us, event | category | flops | bytes accessed | tf_op | source)
XLA Modules:
  0.0 501.5 jit_solution(1524428190305520548)
XLA Ops:
  8.7 1.4 multiply_reduce_fusion.4
  10.2 15.8 %psum.98 = f32[]{:T(128)} all-reduce(f32[]{:T(128)} %multiply_reduce_fusion.4), channel_id=1, replica_groups=mesh['dp'=8,'region'=4] {'dp'}, use_global_device_ids=true, to_apply=%region_1.0 | all-reduce | flops 1 | bytes 8 | tf_op jit(solution)/shard_map/psum | solution.py:27
  26.0 46.5 %psum.99 = f32[]{:T(128)} all-reduce(f32[]{:T(128)} %constant.5.clone.1), channel_id=1, replica_groups=mesh['dp'=8,'region'=4] {'dp','region'}, use_global_device_ids=true, to_apply=%region_2.0 | all-reduce | flops 1 | bytes 8 | tf_op jit(solution)/shard_map/psum | solution.py:27
  75.5 1.1 scatter_custom_fusion.1
  76.6 2.8 fusion.21
  79.4 1.3 scatter_custom_fusion
  80.7 0.8 sub.30
  81.6 32.5 %all-reduce.5.cloned.1.call-done = f32[1024,128]{1,0:T(8,128)} async-done(((f32[1024,128]{1,0:T(8,128)}), f32[1024,128]{1,0:T(8,128)}) %all-reduce.5.cloned.1.call-update) | async-done | bytes 524304 | tf_op jit(solution)/shard_map/psum | solution.py:12
  114.5 75.0 %all-reduce.7.cloned.1.call-done = f32[1024,128]{1,0:T(8,128)} async-done(((f32[1024,128]{1,0:T(8,128)}), f32[1024,128]{1,0:T(8,128)}) %all-reduce.7.cloned.1.call-update) | async-done | bytes 524304 | tf_op jit(solution)/shard_map/psum | solution.py:12
  189.5 1.5 multiply_reduce_fusion.1
  191.1 6.3 %psum.102 = f32[]{:T(128)} all-reduce(f32[]{:T(128)} %multiply_reduce_fusion.1), channel_id=1, replica_groups=mesh['dp'=8,'region'=4] {'region'}, use_global_device_ids=true, to_apply=%region_8.0 | all-reduce | flops 1 | bytes 8 | tf_op jit(solution)/shard_map/psum | solution.py:18
  198.0 0.9 fusion.26
  199.0 6.0 %all_gather.6 = bf16[1024,128]{1,0:T(8,128)(2,1)S(1)} all-gather(bf16[256,128]{1,0:T(8,128)(2,1)S(1)} %fusion.26), channel_id=1, replica_groups=mesh['dp'=8,'region'=4] {'region'}, dimensions={0}, use_global_device_ids=true | all-gather | bytes 327680 | tf_op jit(solution)/shard_map/all_gather | solution.py:23
  205.7 3.4 fusion.16
  209.0 11.5 %psum.103 = bf16[64,128]{1,0:T(8,128)(2,1)S(1)} all-reduce(bf16[64,128]{1,0:T(8,128)(2,1)S(1)} %convert_element_type.46), channel_id=1, replica_groups=mesh['dp'=8,'region'=4] {'region'}, use_global_device_ids=true, to_apply=%region_9.0 | all-reduce | flops 8192 | bytes 32768 | tf_op jit(solution)/shard_map/psum | solution.py:68
  223.1 16.0 %psum.104 = f32[]{:T(128)} all-reduce(f32[]{:T(128)} %multiply_reduce_fusion.3), channel_id=1, replica_groups=mesh['dp'=8,'region'=4] {'dp'}, use_global_device_ids=true, to_apply=%region_11.0 | all-reduce | flops 1 | bytes 8 | tf_op jit(solution)/shard_map/psum | solution.py:27
  239.1 44.3 %psum.105 = f32[]{:T(128)} all-reduce(f32[]{:T(128)} %multiply_reduce_fusion.6), channel_id=1, replica_groups=mesh['dp'=8,'region'=4] {'dp','region'}, use_global_device_ids=true, to_apply=%region_13.0 | all-reduce | flops 1 | bytes 8 | tf_op jit(solution)/shard_map/psum | solution.py:27
  284.8 2.8 fusion.19
  287.7 0.8 scatter_custom_fusion.3
  288.5 1.3 scatter_custom_fusion.2
  289.8 0.9 sub.34
  290.7 31.5 %all-reduce.9.cloned.1.call-done = f32[1024,128]{1,0:T(8,128)} async-done(((f32[1024,128]{1,0:T(8,128)}), f32[1024,128]{1,0:T(8,128)}) %all-reduce.9.cloned.1.call-update) | async-done | bytes 524304 | tf_op jit(solution)/shard_map/psum | solution.py:12
  322.4 75.4 %all-reduce.11.cloned.1.call-done = f32[1024,128]{1,0:T(8,128)} async-done(((f32[1024,128]{1,0:T(8,128)}), f32[1024,128]{1,0:T(8,128)}) %all-reduce.11.cloned.1.call-update) | async-done | bytes 524304 | tf_op jit(solution)/shard_map/psum | solution.py:12
  397.8 1.6 multiply_reduce_fusion
  399.4 6.3 %psum.108 = f32[]{:T(128)} all-reduce(f32[]{:T(128)} %multiply_reduce_fusion), channel_id=1, replica_groups=mesh['dp'=8,'region'=4] {'region'}, use_global_device_ids=true, to_apply=%region_19.0 | all-reduce | flops 1 | bytes 8 | tf_op jit(solution)/shard_map/psum | solution.py:18
  406.4 0.9 fusion.18
  407.3 6.0 %all_gather.7 = bf16[1024,128]{1,0:T(8,128)(2,1)S(1)} all-gather(bf16[256,128]{1,0:T(8,128)(2,1)S(1)} %fusion.18), channel_id=1, replica_groups=mesh['dp'=8,'region'=4] {'region'}, dimensions={0}, use_global_device_ids=true | all-gather | bytes 327680 | tf_op jit(solution)/shard_map/all_gather | solution.py:23
  415.3 3.4 fusion.14
  418.6 11.5 %psum.109 = bf16[64,128]{1,0:T(8,128)(2,1)S(1)} all-reduce(bf16[64,128]{1,0:T(8,128)(2,1)S(1)} %convert_element_type.52), channel_id=1, replica_groups=mesh['dp'=8,'region'=4] {'region'}, use_global_device_ids=true, to_apply=%region_20.0 | all-reduce | flops 8192 | bytes 32768 | tf_op jit(solution)/shard_map/psum | solution.py:68
  430.7 16.0 %psum.110 = f32[]{:T(128)} all-reduce(f32[]{:T(128)} %multiply_reduce_fusion.2), channel_id=1, replica_groups=mesh['dp'=8,'region'=4] {'dp'}, use_global_device_ids=true, to_apply=%region_22.0 | all-reduce | flops 1 | bytes 8 | tf_op jit(solution)/shard_map/psum | solution.py:27
  447.5 44.3 %psum.111 = f32[]{:T(128)} all-reduce(f32[]{:T(128)} %multiply_reduce_fusion.5), channel_id=1, replica_groups=mesh['dp'=8,'region'=4] {'dp','region'}, use_global_device_ids=true, to_apply=%region_24.0 | all-reduce | flops 1 | bytes 8 | tf_op jit(solution)/shard_map/psum | solution.py:27
  493.4 1.6 multiply_add_fusion
  (42 shorter events, 10.3 us)
Async XLA Ops:
  6.5 107.7 %copy-start.3 = (s32[64,2]{0,1:T(2,128)S(1)}, s32[64,2]{0,1:T(2,128)}, u32[]{:S(2)}) copy-start(s32[64,2]{0,1:T(2,128)} %param.8) | copy-start | bytes 1540
  6.5 107.6 %all-reduce.5.cloned.1.call-start = ((), (), s32[]{:S(2)}) async-start(), calls=%async_computation | async-start | bytes 1048576 | tf_op jit(solution)/shard_map/psum | solution.py:12
  80.7 139.8 %copy-start.1 = (f32[64,128]{1,0:T(8,128)S(1)}, f32[64,128]{1,0:T(8,128)}, u32[]{:S(2)}) copy-start(f32[64,128]{1,0:T(8,128)} %param.6) | copy-start | bytes 98308
  80.7 141.6 %copy-start.2 = (f32[32,128]{1,0:T(8,128)S(1)}, f32[32,128]{1,0:T(8,128)}, u32[]{:S(2)}) copy-start(f32[32,128]{1,0:T(8,128)} %param.10) | copy-start | bytes 49156
  81.6 107.9 %all-reduce.7.cloned.1.call-start = ((), (), s32[]{:S(2)}) async-start(), calls=%async_computation.1 | async-start | bytes 1048576 | tf_op jit(solution)/shard_map/psum | solution.py:12
  114.1 208.1 %all-reduce.9.cloned.1.call-start = ((), (), s32[]{:S(2)}) async-start(), calls=%async_computation.2 | async-start | bytes 1048576 | tf_op jit(solution)/shard_map/psum | solution.py:12
  221.1 176.7 %copy-start = (f32[1024,128]{1,0:T(8,128)S(1)}, f32[1024,128]{1,0:T(8,128)}, u32[]{:S(2)}) copy-start(f32[1024,128]{1,0:T(8,128)} %all-reduce.7.cloned.1.call-done) | copy-start | bytes 1572868
  290.7 107.1 %all-reduce.11.cloned.1.call-start = ((), (), s32[]{:S(2)}) async-start(), calls=%async_computation.3 | async-start | bytes 1048576 | tf_op jit(solution)/shard_map/psum | solution.py:12
Sparse Core Ops, SparseCore 0:
  81.7 32.3 all-reduce.4
  117.5 71.9 all-reduce.6
  290.8 31.3 all-reduce.8
  325.9 71.8 all-reduce.10
